TPU v7x, 512 devices: a whole 4x4x16 slice. The times are simulated.
512 devices in a mesh: seq: 128 (over z, x, core), fsdp: 4 (over y).
Axes of the slice: x: 4, y: 4, z: 16, core: 2. Of those that a mesh axis runs over, the one named last changes fastest.
Arguments:
- query_key: bfloat16 [131072, 3072], P(('seq', 'fsdp')), may hold values from -48 to 48
- values: bfloat16 [131072, 3072], P(('seq', 'fsdp')), may hold values from -6 to 6
- cluster_ids: int32 [24, 1024], replicated, may hold values from 0 to 127, as said below
Outputs:
- attended: bfloat16 [131072, 3072], P(('seq', 'fsdp'))
Inputs may be any that keep to these rules, and one draw needn't show every extreme that they name: `cluster_ids`: for every head and cluster at most 10 blocks name that cluster, and for every head some cluster is named by exactly 10 blocks. Among the (head, block) pairs of one group of 6 consecutive heads and one run of 8 blocks starting at a multiple of 8, no cluster is named more than 1 times, and some cluster exactly 1 times; the blocks of one such run name distinct clusters for each head.
All inputs are finite; a program needn't handle non-finite values.
Results may differ from a plain program's by a relative error of at most 0.0027.
Values may be sent and summed in bfloat16 or wider, within the bound.
No kernel may reach another device: no remote copies, remote signals or barrier semaphores. Data moves between devices by JAX's collectives and lax.ppermute only.
A program may use at most 64 MiB of HBM per device.

v0:
```python
import math
import jax
import jax.numpy as jnp
from jax import lax
from jax.sharding import PartitionSpec as P

BLK = 128
masked_score = -1e30


def by_index(source_table, row_index):
    return source_table[jnp.clip(row_index, 0, source_table.shape[0] - 1)]


def softmax_group(key_rows, positions, alive_rows, score_scale):
    scores = jnp.dot(key_rows, key_rows.T, preferred_element_type=jnp.float32) * score_scale
    allowed = alive_rows[None, :] & (positions[None, :] <= positions[:, None])
    scores = jnp.where(allowed, scores, masked_score)
    row_peak = jnp.max(scores, axis=1, keepdims=True)
    weights = jnp.where(allowed, jnp.exp(scores - row_peak), 0.0)
    row_total = jnp.where(alive_rows[:, None], jnp.sum(weights, axis=1, keepdims=True), 1.0)
    return (weights.astype(jnp.bfloat16), row_total)


def shards(query_key, values, cluster_ids):
    seq_count = lax.axis_size("seq")
    group_count = lax.axis_size("fsdp")
    seq_index = lax.axis_index("seq")
    group_index = lax.axis_index("fsdp")
    heads_all = cluster_ids.shape[0]
    group_heads = heads_all // group_count
    head_dim = query_key.shape[1] // heads_all
    tok_rows = query_key.shape[0]
    shard_blocks = group_count * tok_rows // BLK
    all_blocks = cluster_ids.shape[1]
    item_count = group_heads * shard_blocks
    slot_count = max(1, item_count // seq_count)
    capacity = shard_blocks + min(shard_blocks // 4, seq_count - shard_blocks)
    group_rows = capacity * BLK
    send_rows = seq_count * slot_count
    score_scale = 1.0 / math.sqrt(head_dim)
    own_blocks = tok_rows // BLK
    keys_local = lax.all_to_all(query_key, "fsdp", split_axis=1, concat_axis=0, tiled=True)
    value_chunks = values.reshape(tok_rows, group_count, group_heads * head_dim)
    value_chunks, keys_local = lax.optimization_barrier((value_chunks, keys_local))
    by_shift = [lax.dynamic_index_in_dim(value_chunks, group_index, 1, keepdims=False)]
    for shift in range(1, group_count):
        outgoing = lax.dynamic_index_in_dim(
            value_chunks, (group_index + shift) % group_count, 1, keepdims=False
        )
        by_shift.append(
            lax.ppermute(
                outgoing,
                "fsdp",
                [(peer, (peer + shift) % group_count) for peer in range(group_count)],
            )
        )
    source_order = (group_index - jnp.arange(group_count, dtype=jnp.int32)) % group_count
    values_local = jnp.stack(by_shift)[source_order].reshape(
        group_count * tok_rows, group_heads * head_dim
    )

    def into_items(block_data):
        shaped = block_data.reshape(shard_blocks, BLK, group_heads, head_dim)
        return jnp.transpose(shaped, (2, 0, 1, 3)).reshape(item_count, BLK, head_dim)

    key_items = into_items(keys_local)
    value_items = into_items(values_local)
    group_ids = lax.dynamic_slice_in_dim(cluster_ids, group_index * group_heads, group_heads, 0)
    by_source = jnp.transpose(
        group_ids.reshape(group_heads, seq_count, shard_blocks), (1, 0, 2)
    ).reshape(seq_count, item_count)
    own_dest = lax.dynamic_index_in_dim(by_source, seq_index, 0, keepdims=False)
    item_ids = jnp.arange(item_count, dtype=jnp.int32)
    earlier = (own_dest[None, :] == own_dest[:, None]) & (item_ids[None, :] < item_ids[:, None])
    own_pos = own_dest * slot_count + jnp.sum(earlier.astype(jnp.int32), axis=1)
    row_ids = jnp.arange(send_rows, dtype=jnp.int32)
    slot_match = own_pos[None, :] == row_ids[:, None]
    send_pick = jnp.sum(jnp.where(slot_match, item_ids[None, :], 0), axis=1) + item_count * (
        1 - jnp.any(slot_match, axis=1).astype(jnp.int32)
    )
    key_send, group_ids = lax.optimization_barrier((by_index(key_items, send_pick), group_ids))
    arrived_k = lax.all_to_all(key_send, "seq", split_axis=0, concat_axis=0, tiled=True)
    value_send = by_index(value_items, send_pick)
    arrived_k, value_send = lax.optimization_barrier((arrived_k, value_send))
    arrived_v = lax.all_to_all(value_send, "seq", split_axis=0, concat_axis=0, tiled=True)
    by_source = jnp.transpose(
        group_ids.reshape(group_heads, seq_count, shard_blocks), (1, 0, 2)
    ).reshape(seq_count, item_count)
    received_mask = (by_source == seq_index).astype(jnp.int32)
    recv_pos = (
        jnp.arange(seq_count, dtype=jnp.int32)[:, None] * slot_count
        + jnp.cumsum(received_mask, axis=1)
        - received_mask
    )
    recv_by_head = jnp.transpose(
        recv_pos.reshape(seq_count, group_heads, shard_blocks), (1, 0, 2)
    ).reshape(group_heads * all_blocks)
    owned_mask = (group_ids == seq_index).astype(jnp.int32)
    ordinal = jnp.cumsum(owned_mask, axis=1) - owned_mask
    target = jnp.where(
        owned_mask > 0, jnp.arange(group_heads, dtype=jnp.int32)[:, None] * capacity + ordinal, -1
    ).reshape(group_heads * all_blocks)
    slot_ids = jnp.arange(group_heads * capacity, dtype=jnp.int32)
    matches = target[None, :] == slot_ids[:, None]
    present = jnp.any(matches, axis=1)
    source_row = jnp.sum(jnp.where(matches, recv_by_head[None, :], 0), axis=1) + send_rows * (
        1 - present.astype(jnp.int32)
    )
    block_ids = jnp.tile(jnp.arange(all_blocks, dtype=jnp.int32), group_heads)
    block_of = jnp.sum(jnp.where(matches, block_ids[None, :], 0), axis=1)
    key_grouped = by_index(arrived_k, source_row)
    value_grouped = by_index(arrived_v, source_row)
    positions = (block_of[:, None] * BLK + jnp.arange(BLK, dtype=jnp.int32)[None, :]).reshape(
        group_heads, group_rows
    )
    alive_rows = jnp.repeat(present, BLK).reshape(group_heads, group_rows)

    def one_head(operands):
        key_rows, where_at, alive_here = operands
        return softmax_group(key_rows, where_at, alive_here, score_scale)

    weights, totals = lax.map(
        one_head, (key_grouped.reshape(group_heads, group_rows, head_dim), positions, alive_rows)
    )
    value_rows = value_grouped.reshape(group_heads, group_rows, head_dim)
    back_match = source_row[None, :] == row_ids[:, None]
    back_pick = jnp.sum(
        jnp.where(back_match, slot_ids[None, :], 0), axis=1
    ) + group_heads * capacity * (1 - jnp.any(back_match, axis=1).astype(jnp.int32))
    weighted = jnp.einsum("hqk,hkd->hqd", weights, value_rows, preferred_element_type=jnp.float32)
    outputs = (
        (weighted / totals).astype(jnp.bfloat16).reshape(group_heads * capacity, BLK, head_dim)
    )
    returned = lax.all_to_all(
        by_index(outputs, back_pick), "seq", split_axis=0, concat_axis=0, tiled=True
    )
    own_output = by_index(returned, own_pos).reshape(
        group_heads, group_count, own_blocks, BLK, head_dim
    )
    gathered = lax.all_to_all(
        jnp.swapaxes(own_output, 0, 1), "fsdp", split_axis=0, concat_axis=0, tiled=True
    )
    token_major = jnp.transpose(gathered, (2, 3, 0, 1, 4))
    return token_major.reshape(tok_rows, heads_all * head_dim)


def solution(mesh):
    placed = (P(("seq", "fsdp"), None), P(("seq", "fsdp"), None), P())
    return jax.shard_map(
        shards, mesh=mesh, in_specs=placed, out_specs=P(("seq", "fsdp"), None), check_vma=False
    )
```

profile of v0, /device:TPU:70, one launch (start us, length us, event | category | flops | bytes accessed | tf_op | source)
XLA Modules:
  0.0 684.2 jit_solution(3121798839654760957)
XLA Ops:
  0.0 2.6 copy.60
  2.6 4.6 all-to-all-start
  8.2 1.1 copy.64
  9.8 1.6 copy.59
  11.8 16.1 %all-to-all-done = bf16[256,4,768]{0,2,1:T(8,128)(2,1)S(1)} async-done(((bf16[256,4,768]{0,2,1:T(8,128)(2,1)}), bf16[256,4,768]{0,2,1:T(8,128)(2,1)S(1)}, u32[]{:S(2)}, u32[]{:S(2)}) %all-to-all-start) | async-done | bytes 1572896 | tf_op jit(solution)/shard_map/all_to_all | solution.py:43
  29.8 1.1 copy.63
  31.0 3.1 gather_fusion
  34.1 18.9 %all-to-all-start.1 = ((bf16[128,128,128]{2,1,0:T(8,128)(2,1)}), bf16[128,128,128]{2,1,0:T(8,128)(2,1)}, u32[]{:S(2)}, u32[]{:S(2)}) async-start(bf16[128,128,128]{2,1,0:T(8,128)(2,1)} %gather_fusion), calls=%async_computation.1 | async-start | bytes 8388608 | tf_op jit(solution)/shard_map/all_to_all | solution.py:83
  53.3 1.7 reduce-window.6
  56.7 2.5 collective-permute-start
  59.4 4.0 collective-permute-start.1
  63.5 2.5 collective-permute-start.2
  67.9 11.5 %collective-permute-done = bf16[256,768]{1,0:T(8,128)(2,1)S(1)} collective-permute-done((bf16[256,768]{1,0:T(8,128)(2,1)S(1)}, bf16[256,768]{1,0:T(8,128)(2,1)S(1)}, u32[]{:S(2)}, u32[]{:S(2)}) %collective-permute-start) | collective-permute-done | bytes 393248 | tf_op jit(solution)/shard_map/ppermute | solution.py:52
  79.4 2.7 collective-permute-done.2
  82.9 1.2 pad_maximum_fusion
  86.4 1.1 copy.73
  87.5 3.1 gather_fusion.2
  90.7 150.5 %all-to-all-done.1 = bf16[128,128,128]{2,1,0:T(8,128)(2,1)} async-done(((bf16[128,128,128]{2,1,0:T(8,128)(2,1)}), bf16[128,128,128]{2,1,0:T(8,128)(2,1)}, u32[]{:S(2)}, u32[]{:S(2)}) %all-to-all-start.1) | async-done | bytes 4194336 | tf_op jit(solution)/shard_map/all_to_all | solution.py:83
  241.2 8.9 %all-to-all-start.2 = ((bf16[128,128,128]{2,1,0:T(8,128)(2,1)}), bf16[128,128,128]{2,1,0:T(8,128)(2,1)}, u32[]{:S(2)}, u32[]{:S(2)}) async-start(bf16[128,128,128]{2,1,0:T(8,128)(2,1)} %gather_fusion.2), calls=%async_computation.2 | async-start | bytes 8388608 | tf_op jit(solution)/shard_map/all_to_all | solution.py:86
  250.2 3.1 gather_fusion.3
  253.3 46.0 %while.12 = (s32[]{:T(128)}, bf16[6,1280,1280]{1,2,0:T(8,128)(2,1)}, f32[6,1280,1]{1,0,2:T(8,128)S(1)}, pred[6,1280]{1,0:T(8,128)(4,1)S(1)}, s32[6,1280]{1,0:T(8...) while((s32[]{:T(128)}, bf16[6,1280,1280]{1,2,0:T(8,128)(2,1)}, ...), condition=%wide.region_12.13_spmd, body=%wide.region_9.12_spmd.sunk | while | flops 444005120 | bytes 23367272 | solution.py:123
  253.4 1.7 fusion.30
  255.1 3.4 fusion.31
  258.5 2.3 fusion.32
  261.0 1.7 fusion.30
  262.7 3.4 fusion.31
  266.1 2.3 fusion.32
  268.7 1.7 fusion.30
  270.4 3.4 fusion.31
  273.9 2.3 fusion.32
  276.4 1.7 fusion.30
  278.1 3.4 fusion.31
  281.5 2.3 fusion.32
  284.1 1.7 fusion.30
  285.8 3.4 fusion.31
  289.2 2.3 fusion.32
  291.7 1.7 fusion.30
  293.5 3.4 fusion.31
  296.8 2.3 fusion.32
  299.3 138.9 %all-to-all-done.2 = bf16[128,128,128]{2,1,0:T(8,128)(2,1)} async-done(((bf16[128,128,128]{2,1,0:T(8,128)(2,1)}), bf16[128,128,128]{2,1,0:T(8,128)(2,1)}, u32[]{:S(2)}, u32[]{:S(2)}) %all-to-all-start.2) | async-done | bytes 4194336 | tf_op jit(solution)/shard_map/all_to_all | solution.py:86
  438.2 4.4 gather_fusion.4
  442.6 11.0 %divide_convert_fusion = bf16[6,1280,128]{2,1,0:T(8,128)(2,1)S(1)} fusion(bf16[6,1280,1280]{1,2,0:T(8,128)(2,1)} %get-tuple-element.49, bf16[6,1280,128]{2,1,0:T(8,128)(2,1)} %bitcast.118, f32[6,1280]{1,0:T(8,128)S(1)} %bitcast.134), kind=kOutput, calls=%fused_computation.22 | convolution fusion | flops 2518548480 | bytes 23623680 | tf_op jit(solution)/shard_map/hqk,hkd->hqd/dot_general | solution.py:131
  453.6 3.1 gather_fusion.5
  456.6 8.9 %all-to-all-start.3 = ((bf16[128,128,128]{2,1,0:T(8,128)(2,1)}), bf16[128,128,128]{2,1,0:T(8,128)(2,1)}, u32[]{:S(2)}, u32[]{:S(2)}) async-start(bf16[128,128,128]{2,1,0:T(8,128)(2,1)} %gather_fusion.5), calls=%async_computation.3 | async-start | bytes 8388608 | tf_op jit(solution)/shard_map/all_to_all | solution.py:135
  465.6 188.1 %all-to-all-done.3 = bf16[128,128,128]{2,1,0:T(8,128)(2,1)} async-done(((bf16[128,128,128]{2,1,0:T(8,128)(2,1)}), bf16[128,128,128]{2,1,0:T(8,128)(2,1)}, u32[]{:S(2)}, u32[]{:S(2)}) %all-to-all-start.3) | async-done | bytes 4194336 | tf_op jit(solution)/shard_map/all_to_all | solution.py:135
  653.7 3.0 gather_fusion.6
  656.9 23.6 %all_to_all.39 = bf16[4,6,2,128,128]{4,3,2,1,0:T(8,128)(2,1)S(1)} all-to-all(bf16[4,6,2,128,128]{4,3,2,1,0:T(8,128)(2,1)S(1)} %copy.77), channel_id=1, replica_groups=mesh['seq'=128,'fsdp'=4] {'fsdp'}, dimensions={0} | all-to-all | bytes 3145728 | tf_op jit(solution)/shard_map/all_to_all | solution.py:141
  681.6 2.6 reshape.391
  (97 shorter events, 13.2 us)
Async XLA Ops:
  0.0 7.2 %copy-start = (s32[24,1024]{1,0:T(8,128)S(1)}, s32[24,1024]{1,0:T(8,128)}, u32[]{:S(2)}) copy-start(s32[24,1024]{1,0:T(8,128)} %param.7) | copy-start | bytes 294916
  2.6 7.2 %copy-start.3 = (bf16[256,3072]{1,0:T(8,128)(2,1)S(1)}, bf16[256,3072]{1,0:T(8,128)(2,1)}, u32[]{:S(2)}) copy-start(bf16[256,3072]{1,0:T(8,128)(2,1)} %param.6) | copy-start | bytes 4718596
  2.6 25.3 %all-to-all-start = ((bf16[256,4,768]{0,2,1:T(8,128)(2,1)}), bf16[256,4,768]{0,2,1:T(8,128)(2,1)S(1)}, u32[]{:S(2)}, u32[]{:S(2)}) async-start(bf16[256,4,768]{0,2,1:T(8,128)(2,1)} %bitcast.4), calls=%async_computation | async-start | bytes 3145728 | tf_op jit(solution)/shard_map/all_to_all | solution.py:43
  34.1 207.1 %all-to-all-start.1 = ((bf16[128,128,128]{2,1,0:T(8,128)(2,1)}), bf16[128,128,128]{2,1,0:T(8,128)(2,1)}, u32[]{:S(2)}, u32[]{:S(2)}) async-start(bf16[128,128,128]{2,1,0:T(8,128)(2,1)} %gather_fusion), calls=%async_computation.1 | async-start | bytes 8388608 | tf_op jit(solution)/shard_map/all_to_all | solution.py:83
  53.0 3.4 copy-start.2
  56.7 22.7 %collective-permute-start = (bf16[256,768]{1,0:T(8,128)(2,1)S(1)}, bf16[256,768]{1,0:T(8,128)(2,1)S(1)}, u32[]{:S(2)}, u32[]{:S(2)}) collective-permute-start(bf16[256,768]{1,0:T(8,128)(2,1)S(1)} %bitcast.124), channel_id=1, source_target_pairs={{0,1},{1,2},{2,3},{3,0},{4,5},{5,6},{6,7},{7,4},{8,9},{9,10},{10,1... | collective-permute-start | bytes 1179656 | tf_op jit(solution)/shard_map/ppermute | solution.py:52
  59.4 20.0 %collective-permute-start.1 = (bf16[256,768]{1,0:T(8,128)(2,1)S(1)}, bf16[256,768]{1,0:T(8,128)(2,1)S(1)}, u32[]{:S(2)}, u32[]{:S(2)}) collective-permute-start(bf16[256,768]{1,0:T(8,128)(2,1)S(1)} %bitcast.125), channel_id=1, source_target_pairs={{0,2},{1,3},{2,0},{3,1},{4,6},{5,7},{6,4},{7,5},{8,10},{9,11},{10,... | collective-permute-start | bytes 1179656 | tf_op jit(solution)/shard_map/ppermute | solution.py:52
  63.5 18.6 %collective-permute-start.2 = (bf16[256,768]{1,0:T(8,128)(2,1)S(1)}, bf16[256,768]{1,0:T(8,128)(2,1)S(1)}, u32[]{:S(2)}, u32[]{:S(2)}) collective-permute-start(bf16[256,768]{1,0:T(8,128)(2,1)S(1)} %bitcast.126), channel_id=1, source_target_pairs={{0,3},{1,0},{2,1},{3,2},{4,7},{5,4},{6,5},{7,6},{8,11},{9,8},{10,9... | collective-permute-start | bytes 1179656 | tf_op jit(solution)/shard_map/ppermute | solution.py:52
  82.1 0.7 copy-start.4
  241.2 197.1 %all-to-all-start.2 = ((bf16[128,128,128]{2,1,0:T(8,128)(2,1)}), bf16[128,128,128]{2,1,0:T(8,128)(2,1)}, u32[]{:S(2)}, u32[]{:S(2)}) async-start(bf16[128,128,128]{2,1,0:T(8,128)(2,1)} %gather_fusion.2), calls=%async_computation.2 | async-start | bytes 8388608 | tf_op jit(solution)/shard_map/all_to_all | solution.py:86
  456.6 197.1 %all-to-all-start.3 = ((bf16[128,128,128]{2,1,0:T(8,128)(2,1)}), bf16[128,128,128]{2,1,0:T(8,128)(2,1)}, u32[]{:S(2)}, u32[]{:S(2)}) async-start(bf16[128,128,128]{2,1,0:T(8,128)(2,1)} %gather_fusion.5), calls=%async_computation.3 | async-start | bytes 8388608 | tf_op jit(solution)/shard_map/all_to_all | solution.py:135
  680.5 3.7 copy-start.1
where the time goes:
time: 685 us; the launch traced here: 684 us
  waiting for transfers between devices  508 us (74%)
  starting transfers between devices  50.4 us (7%)
  local copies, waits for them, and re-layouts  40.9 us (6%)
  other arithmetic  39.3 us (6%)
  blocking collectives  23.6 us (3%)
  matrix products  21.4 us (3%)
    all_to_all x1, waiting for transfers between devices, shards(): lax.all_to_all(by_index(outputs, back_pick), 'seq', split_axis=0, concat_...  188 us
    all_to_all x1, waiting for transfers between devices, shards(): lax.all_to_all(key_send, 'seq', split_axis=0, concat_axis=0, tiled=True)  151 us
    all_to_all x1, waiting for transfers between devices, shards(): lax.all_to_all(value_send, 'seq', split_axis=0, concat_axis=0, tiled=True)  139 us
    all_to_all x1, blocking collectives, shards(): lax.all_to_all(jnp.swapaxes(own_output, 0, 1), 'fsdp', split_axis=0, conc...  23.6 us
    dynamic_update_slice x12, other arithmetic, shards(): lax.map(one_head, (key_grouped.reshape(group_heads, group_rows, head_dim)...  20.4 us
    gather x6, local copies, waits for them, and re-layouts, by_index(): return source_table[jnp.clip(row_index, 0, source_table.shape[0] - 1)]  19.8 us
    all_to_all x1, starting transfers between devices, shards(): lax.all_to_all(key_send, 'seq', split_axis=0, concat_axis=0, tiled=True)  18.9 us
    all_to_all x1, waiting for transfers between devices, shards(): lax.all_to_all(query_key, 'fsdp', split_axis=1, concat_axis=0, tiled=True)  16.1 us
  transfers between devices with their start and end apart: 7, of which 6 were waited for; matrix products, arithmetic and copies ran while one was open for 10% of the time, Pallas kernels for 0%

commit v1 on v0

--- a/solution.py
+++ b/solution.py
@@ -6,6 +6,26 @@
 
 BLK = 128
 masked_score = -1e30
+
+
+def wait_the_frame(tile_in, where_dim, dim_no):
+    next_value, far_arr = (lax.axis_size("fsdp"), lax.axis_index("fsdp"))
+    block_out = tile_in.shape[where_dim] // next_value
+    block_last = list(tile_in.shape)
+    block_last[where_dim] = block_out
+    mixed_arr = block_last[dim_no]
+    block_last[dim_no] = mixed_arr * next_value
+    tile_out = jnp.zeros(block_last, tile_in.dtype)
+    for b in range(next_value):
+        upper = lax.dynamic_slice_in_dim(
+            tile_in, (far_arr ^ b) * block_out, block_out, axis=where_dim
+        )
+        if b:
+            upper = lax.ppermute(upper, "fsdp", tuple(((ii, ii ^ b) for ii in range(next_value))))
+        tile_out = lax.dynamic_update_slice_in_dim(
+            tile_out, upper, (far_arr ^ b) * mixed_arr, axis=dim_no
+        )
+    return tile_out
 
 
 def by_index(source_table, row_index):
@@ -138,9 +158,7 @@
     own_output = by_index(returned, own_pos).reshape(
         group_heads, group_count, own_blocks, BLK, head_dim
     )
-    gathered = lax.all_to_all(
-        jnp.swapaxes(own_output, 0, 1), "fsdp", split_axis=0, concat_axis=0, tiled=True
-    )
+    gathered = wait_the_frame(jnp.swapaxes(own_output, 0, 1), 0, 0)
     token_major = jnp.transpose(gathered, (2, 3, 0, 1, 4))
     return token_major.reshape(tok_rows, heads_all * head_dim)
 

time: 685 us -> 690 us (level)
  blocking collectives: 23.6 us -> 0 us
  waiting for transfers between devices: 508 us -> 523 us
  starting transfers between devices: 50.4 us -> 60.8 us
    all_to_all x1 -> x0, blocking collectives: 23.6 us -> none  [shards(): lax.all_to_all(jnp.swapaxes(own_output, 0, 1), 'fsdp', split_axis=0, conc...]
    ppermute x0 -> x3, waiting for transfers between devices: none -> 15.5 us  [wait_the_frame(): lax.ppermute(upper, 'fsdp', tuple(((ii, ii ^ b) for ii in range(next_valu...]
    ppermute x0 -> x3, starting transfers between devices: none -> 10.4 us  [wait_the_frame(): lax.ppermute(upper, 'fsdp', tuple(((ii, ii ^ b) for ii in range(next_valu...]
  transfers between devices with their start and end apart: 7 -> 10, of which waited for: 6 -> 9; matrix products, arithmetic and copies ran while one was open for 10% -> 10% of each run, Pallas kernels for 0% -> 0%
where the time goes in v1:
time: 690 us; the launch traced here: 689 us
  waiting for transfers between devices  523 us (76%)
  starting transfers between devices  60.8 us (9%)
  local copies, waits for them, and re-layouts  43.4 us (6%)
  other arithmetic  39.3 us (6%)
  matrix products  21.4 us (3%)
    all_to_all x1, waiting for transfers between devices, shards(): lax.all_to_all(by_index(outputs, back_pick), 'seq', split_axis=0, concat_...  188 us
    all_to_all x1, waiting for transfers between devices, shards(): lax.all_to_all(key_send, 'seq', split_axis=0, concat_axis=0, tiled=True)  151 us
    all_to_all x1, waiting for transfers between devices, shards(): lax.all_to_all(value_send, 'seq', split_axis=0, concat_axis=0, tiled=True)  139 us
    dynamic_update_slice x12, other arithmetic, shards(): lax.map(one_head, (key_grouped.reshape(group_heads, group_rows, head_dim)...  20.4 us
    gather x6, local copies, waits for them, and re-layouts, by_index(): return source_table[jnp.clip(row_index, 0, source_table.shape[0] - 1)]  19.8 us
    all_to_all x1, starting transfers between devices, shards(): lax.all_to_all(key_send, 'seq', split_axis=0, concat_axis=0, tiled=True)  18.9 us
    all_to_all x1, waiting for transfers between devices, shards(): lax.all_to_all(query_key, 'fsdp', split_axis=1, concat_axis=0, tiled=True)  16.1 us
    ppermute x3, waiting for transfers between devices, wait_the_frame(): lax.ppermute(upper, 'fsdp', tuple(((ii, ii ^ b) for ii in range(next_valu...  15.5 us
  transfers between devices with their start and end apart: 10, of which 9 were waited for; matrix products, arithmetic and copies ran while one was open for 10% of the time, Pallas kernels for 0%

profile of v1, /device:TPU:70, one launch (start us, length us, event | category | flops | bytes accessed | tf_op | source)
XLA Modules:
  0.0 689.1 jit_solution(1056705197599896577)
XLA Ops:
  0.0 2.6 copy.49
  2.6 4.6 all-to-all-start
  9.8 1.6 copy.48
  11.8 16.1 %all-to-all-done = bf16[256,4,768]{0,2,1:T(8,128)(2,1)S(1)} async-done(((bf16[256,4,768]{0,2,1:T(8,128)(2,1)}), bf16[256,4,768]{0,2,1:T(8,128)(2,1)S(1)}, u32[]{:S(2)}, u32[]{:S(2)}) %all-to-all-start) | async-done | bytes 1572896 | tf_op jit(solution)/shard_map/all_to_all | solution.py:63
  31.0 3.1 gather_fusion
  34.1 18.9 %all-to-all-start.1 = ((bf16[128,128,128]{2,1,0:T(8,128)(2,1)}), bf16[128,128,128]{2,1,0:T(8,128)(2,1)}, u32[]{:S(2)}, u32[]{:S(2)}) async-start(bf16[128,128,128]{2,1,0:T(8,128)(2,1)} %gather_fusion), calls=%async_computation.1 | async-start | bytes 8388608 | tf_op jit(solution)/shard_map/all_to_all | solution.py:103
  53.3 1.7 reduce-window.6
  56.7 2.5 collective-permute-start
  59.4 4.0 collective-permute-start.1
  63.5 2.5 collective-permute-start.2
  67.9 11.5 %collective-permute-done = bf16[256,768]{1,0:T(8,128)(2,1)S(1)} collective-permute-done((bf16[256,768]{1,0:T(8,128)(2,1)S(1)}, bf16[256,768]{1,0:T(8,128)(2,1)S(1)}, u32[]{:S(2)}, u32[]{:S(2)}) %collective-permute-start) | collective-permute-done | bytes 393248 | tf_op jit(solution)/shard_map/ppermute | solution.py:72
  79.4 2.7 collective-permute-done.2
  87.5 3.1 gather_fusion.2
  90.7 150.5 %all-to-all-done.1 = bf16[128,128,128]{2,1,0:T(8,128)(2,1)} async-done(((bf16[128,128,128]{2,1,0:T(8,128)(2,1)}), bf16[128,128,128]{2,1,0:T(8,128)(2,1)}, u32[]{:S(2)}, u32[]{:S(2)}) %all-to-all-start.1) | async-done | bytes 4194336 | tf_op jit(solution)/shard_map/all_to_all | solution.py:103
  241.2 8.9 %all-to-all-start.2 = ((bf16[128,128,128]{2,1,0:T(8,128)(2,1)}), bf16[128,128,128]{2,1,0:T(8,128)(2,1)}, u32[]{:S(2)}, u32[]{:S(2)}) async-start(bf16[128,128,128]{2,1,0:T(8,128)(2,1)} %gather_fusion.2), calls=%async_computation.2 | async-start | bytes 8388608 | tf_op jit(solution)/shard_map/all_to_all | solution.py:106
  250.2 3.1 gather_fusion.3
  253.3 46.0 %while.12 = (s32[]{:T(128)}, bf16[6,1280,1280]{1,2,0:T(8,128)(2,1)}, f32[6,1280,1]{1,0,2:T(8,128)S(1)}, pred[6,1280]{1,0:T(8,128)(4,1)S(1)}, s32[6,1280]{1,0:T(8...) while((s32[]{:T(128)}, bf16[6,1280,1280]{1,2,0:T(8,128)(2,1)}, ...), condition=%wide.region_12.13_spmd, body=%wide.region_9.12_spmd.sunk | while | flops 444005120 | bytes 23367272 | solution.py:143
  253.4 1.7 fusion.30
  255.1 3.4 fusion.31
  258.5 2.3 fusion.32
  261.0 1.7 fusion.30
  262.7 3.4 fusion.31
  266.1 2.3 fusion.32
  268.7 1.7 fusion.30
  270.4 3.4 fusion.31
  273.9 2.3 fusion.32
  276.4 1.7 fusion.30
  278.1 3.4 fusion.31
  281.5 2.3 fusion.32
  284.1 1.7 fusion.30
  285.8 3.4 fusion.31
  289.2 2.3 fusion.32
  291.7 1.7 fusion.30
  293.5 3.4 fusion.31
  296.8 2.3 fusion.32
  299.3 138.9 %all-to-all-done.2 = bf16[128,128,128]{2,1,0:T(8,128)(2,1)} async-done(((bf16[128,128,128]{2,1,0:T(8,128)(2,1)}), bf16[128,128,128]{2,1,0:T(8,128)(2,1)}, u32[]{:S(2)}, u32[]{:S(2)}) %all-to-all-start.2) | async-done | bytes 4194336 | tf_op jit(solution)/shard_map/all_to_all | solution.py:106
  438.2 4.4 gather_fusion.4
  442.6 11.0 %divide_convert_fusion = bf16[6,1280,128]{2,1,0:T(8,128)(2,1)S(1)} fusion(bf16[6,1280,1280]{1,2,0:T(8,128)(2,1)} %get-tuple-element.49, bf16[6,1280,128]{2,1,0:T(8,128)(2,1)} %bitcast.129, f32[6,1280]{1,0:T(8,128)S(1)} %bitcast.148), kind=kOutput, calls=%fused_computation.22 | convolution fusion | flops 2518548480 | bytes 23623680 | tf_op jit(solution)/shard_map/hqk,hkd->hqd/dot_general | solution.py:151
  453.6 3.1 gather_fusion.5
  456.6 9.0 %all-to-all-start.3 = ((bf16[128,128,128]{2,1,0:T(8,128)(2,1)}), bf16[128,128,128]{2,1,0:T(8,128)(2,1)}, u32[]{:S(2)}, u32[]{:S(2)}) async-start(bf16[128,128,128]{2,1,0:T(8,128)(2,1)} %gather_fusion.5), calls=%async_computation.3 | async-start | bytes 8388608 | tf_op jit(solution)/shard_map/all_to_all | solution.py:155
  465.6 188.1 %all-to-all-done.3 = bf16[128,128,128]{2,1,0:T(8,128)(2,1)} async-done(((bf16[128,128,128]{2,1,0:T(8,128)(2,1)}), bf16[128,128,128]{2,1,0:T(8,128)(2,1)}, u32[]{:S(2)}, u32[]{:S(2)}) %all-to-all-start.3) | async-done | bytes 4194336 | tf_op jit(solution)/shard_map/all_to_all | solution.py:155
  653.7 3.0 gather_fusion.6
  657.3 2.5 collective-permute-start.3
  660.2 4.0 collective-permute-start.4
  665.1 4.0 collective-permute-start.5
  671.5 7.8 %collective-permute-done.4 = bf16[1,6,2,128,128]{3,2,4,1,0:T(2,128)(2,1)S(1)} collective-permute-done((bf16[1,6,2,128,128]{3,2,4,1,0:T(2,128)(2,1)S(1)}, bf16[1,6,2,128,128]{3,2,4,1,0:T(2,128)(2,1)S(1)}, u32[]{:S(2)}, u32[]{:S(2)}) %collective-permute-start.4) | collective-permute-done | bytes 393248 | tf_op jit(solution)/shard_map/ppermute | solution.py:24
  679.7 7.2 %collective-permute-done.5 = bf16[1,6,2,128,128]{3,2,4,1,0:T(2,128)(2,1)S(1)} collective-permute-done((bf16[1,6,2,128,128]{3,2,4,1,0:T(2,128)(2,1)S(1)}, bf16[1,6,2,128,128]{3,2,4,1,0:T(2,128)(2,1)S(1)}, u32[]{:S(2)}, u32[]{:S(2)}) %collective-permute-start.5) | collective-permute-done | bytes 393248 | tf_op jit(solution)/shard_map/ppermute | solution.py:24
  687.4 1.7 copy.70
  (111 shorter events, 21.6 us)
Async XLA Ops:
  0.0 7.2 %copy-start = (s32[24,1024]{1,0:T(8,128)S(1)}, s32[24,1024]{1,0:T(8,128)}, u32[]{:S(2)}) copy-start(s32[24,1024]{1,0:T(8,128)} %param.7) | copy-start | bytes 294916
  2.6 7.2 %copy-start.3 = (bf16[256,3072]{1,0:T(8,128)(2,1)S(1)}, bf16[256,3072]{1,0:T(8,128)(2,1)}, u32[]{:S(2)}) copy-start(bf16[256,3072]{1,0:T(8,128)(2,1)} %param.6) | copy-start | bytes 4718596
  2.6 25.3 %all-to-all-start = ((bf16[256,4,768]{0,2,1:T(8,128)(2,1)}), bf16[256,4,768]{0,2,1:T(8,128)(2,1)S(1)}, u32[]{:S(2)}, u32[]{:S(2)}) async-start(bf16[256,4,768]{0,2,1:T(8,128)(2,1)} %bitcast.4), calls=%async_computation | async-start | bytes 3145728 | tf_op jit(solution)/shard_map/all_to_all | solution.py:63
  34.1 207.1 %all-to-all-start.1 = ((bf16[128,128,128]{2,1,0:T(8,128)(2,1)}), bf16[128,128,128]{2,1,0:T(8,128)(2,1)}, u32[]{:S(2)}, u32[]{:S(2)}) async-start(bf16[128,128,128]{2,1,0:T(8,128)(2,1)} %gather_fusion), calls=%async_computation.1 | async-start | bytes 8388608 | tf_op jit(solution)/shard_map/all_to_all | solution.py:103
  53.0 3.4 copy-start.2
  56.7 22.7 %collective-permute-start = (bf16[256,768]{1,0:T(8,128)(2,1)S(1)}, bf16[256,768]{1,0:T(8,128)(2,1)S(1)}, u32[]{:S(2)}, u32[]{:S(2)}) collective-permute-start(bf16[256,768]{1,0:T(8,128)(2,1)S(1)} %bitcast.135), channel_id=1, source_target_pairs={{0,1},{1,2},{2,3},{3,0},{4,5},{5,6},{6,7},{7,4},{8,9},{9,10},{10,1... | collective-permute-start | bytes 1179656 | tf_op jit(solution)/shard_map/ppermute | solution.py:72
  59.4 20.0 %collective-permute-start.1 = (bf16[256,768]{1,0:T(8,128)(2,1)S(1)}, bf16[256,768]{1,0:T(8,128)(2,1)S(1)}, u32[]{:S(2)}, u32[]{:S(2)}) collective-permute-start(bf16[256,768]{1,0:T(8,128)(2,1)S(1)} %bitcast.136), channel_id=1, source_target_pairs={{0,2},{1,3},{2,0},{3,1},{4,6},{5,7},{6,4},{7,5},{8,10},{9,11},{10,... | collective-permute-start | bytes 1179656 | tf_op jit(solution)/shard_map/ppermute | solution.py:72
  63.5 18.6 %collective-permute-start.2 = (bf16[256,768]{1,0:T(8,128)(2,1)S(1)}, bf16[256,768]{1,0:T(8,128)(2,1)S(1)}, u32[]{:S(2)}, u32[]{:S(2)}) collective-permute-start(bf16[256,768]{1,0:T(8,128)(2,1)S(1)} %bitcast.137), channel_id=1, source_target_pairs={{0,3},{1,0},{2,1},{3,2},{4,7},{5,4},{6,5},{7,6},{8,11},{9,8},{10,9... | collective-permute-start | bytes 1179656 | tf_op jit(solution)/shard_map/ppermute | solution.py:72
  82.1 0.7 copy-start.4
  241.2 197.1 %all-to-all-start.2 = ((bf16[128,128,128]{2,1,0:T(8,128)(2,1)}), bf16[128,128,128]{2,1,0:T(8,128)(2,1)}, u32[]{:S(2)}, u32[]{:S(2)}) async-start(bf16[128,128,128]{2,1,0:T(8,128)(2,1)} %gather_fusion.2), calls=%async_computation.2 | async-start | bytes 8388608 | tf_op jit(solution)/shard_map/all_to_all | solution.py:106
  456.6 197.1 %all-to-all-start.3 = ((bf16[128,128,128]{2,1,0:T(8,128)(2,1)}), bf16[128,128,128]{2,1,0:T(8,128)(2,1)}, u32[]{:S(2)}, u32[]{:S(2)}) async-start(bf16[128,128,128]{2,1,0:T(8,128)(2,1)} %gather_fusion.5), calls=%async_computation.3 | async-start | bytes 8388608 | tf_op jit(solution)/shard_map/all_to_all | solution.py:155
  657.3 13.9 %collective-permute-start.3 = (bf16[1,6,2,128,128]{3,2,4,1,0:T(2,128)(2,1)S(1)}, bf16[1,6,2,128,128]{3,2,4,1,0:T(2,128)(2,1)S(1)}, u32[]{:S(2)}, u32[]{:S(2)}) collective-permute-start(bf16[1,6,2,128,128]{3,2,4,1,0:T(2,128)(2,1)S(1)} %bitcast.140), channel_id=1, source_target_pairs={{0,1},{1,0},{2,3},{3,2},{4,5},{5,4},{6,7},{7,6},{8,9},{9,8},{10,11... | collective-permute-start | bytes 1179656 | tf_op jit(solution)/shard_map/ppermute | solution.py:24
  660.2 19.1 %collective-permute-start.4 = (bf16[1,6,2,128,128]{3,2,4,1,0:T(2,128)(2,1)S(1)}, bf16[1,6,2,128,128]{3,2,4,1,0:T(2,128)(2,1)S(1)}, u32[]{:S(2)}, u32[]{:S(2)}) collective-permute-start(bf16[1,6,2,128,128]{3,2,4,1,0:T(2,128)(2,1)S(1)} %bitcast.138), channel_id=1, source_target_pairs={{0,2},{1,3},{2,0},{3,1},{4,6},{5,7},{6,4},{7,5},{8,10},{9,11},{10,... | collective-permute-start | bytes 1179656 | tf_op jit(solution)/shard_map/ppermute | solution.py:24
  665.1 21.8 %collective-permute-start.5 = (bf16[1,6,2,128,128]{3,2,4,1,0:T(2,128)(2,1)S(1)}, bf16[1,6,2,128,128]{3,2,4,1,0:T(2,128)(2,1)S(1)}, u32[]{:S(2)}, u32[]{:S(2)}) collective-permute-start(bf16[1,6,2,128,128]{3,2,4,1,0:T(2,128)(2,1)S(1)} %bitcast.139), channel_id=1, source_target_pairs={{0,3},{1,2},{2,1},{3,0},{4,7},{5,6},{6,5},{7,4},{8,11},{9,10},{10,... | collective-permute-start | bytes 1179656 | tf_op jit(solution)/shard_map/ppermute | solution.py:24
  687.2 2.0 copy-start.1
